TPU v7x, 512 devices: a whole 4x4x16 slice. The times are simulated.
512 devices in a mesh: grp: 4 (over y), seq: 32 (over z, core), mp: 4 (over x).
Axes of the slice: x: 4, y: 4, z: 16, core: 2. Of those that a mesh axis runs over, the one named last changes fastest.
Arguments:
- queries: bfloat16 [4, 4096, 2048], P('grp', 'seq', 'mp'), may hold values from -16 to 16
- d_out: bfloat16 [4, 4096, 2048], P('grp', 'seq', 'mp'), may hold values from -6 to 6
- neighbour_kv: bfloat16 [4, 256, 128, 2, 2048], P('grp', 'seq', None, None, 'mp'), may hold values from -16 to 16
- target: int32 [4, 256], P('grp', 'seq'), may hold values from -1 to 127, as said below
- bias: float32 [16, 191], P('mp'), may hold values from -6 to 6
Outputs:
- attended: bfloat16 [4, 4096, 2048], P('grp', 'seq', 'mp')
- d_query: bfloat16 [4, 4096, 2048], P('grp', 'seq', 'mp')
- d_kv: bfloat16 [4, 256, 128, 2, 2048], P('grp', 'seq', None, None, 'mp')
- d_bias: float32 [16, 191], P('mp')
Inputs may be any that keep to these rules, and one draw needn't show every extreme that they name: `target`: in each group every entry 0..127 stands in exactly one slot and -1 marks an empty slot. The slots of one index of seq hold at most 1 entries e with the same e // 4, and some index reaches that; some index of seq holds 8 entries.
All inputs are finite; a program needn't handle non-finite values.
Results may differ from a plain program's by a relative error of at most 0.011.
Values may be sent and summed in bfloat16 or wider, within the bound.
No kernel may reach another device: no remote copies, remote signals or barrier semaphores. Data moves between devices by JAX's collectives and lax.ppermute only.
A program may use at most 128 MiB of HBM per device.

v0:
```python
import jax
import jax.numpy as jnp
from jax import lax
from jax.sharding import PartitionSpec as P

STRETCH = 64
NB_LEN = 128
SEQ_LEN = 2048


def passed_along(block, axis, distance):
    devices = range(lax.axis_size(axis))
    route = [(i - distance, i) for i in devices if i - distance in devices]
    return lax.ppermute(block, axis, route)


def bias_grid(lookup, row_count, col_count):
    head_num = lookup.shape[0]
    span = row_count + col_count
    padded = jnp.pad(lookup, ((0, 0), (0, 1)))
    flattened = jnp.tile(padded, (1, row_count))
    flattened = jnp.pad(flattened, ((0, 0), (0, row_count)))
    shaped = flattened.reshape(head_num, row_count, span + 1)[:, :, :col_count]
    return shaped[:, :, ::-1]


def bias_fold(grads):
    head_num, row_count, col_count = grads.shape
    turned = grads[:, :, ::-1]
    padded = jnp.pad(turned, ((0, 0), (0, 0), (0, row_count)))
    flattened = padded.reshape(head_num, row_count * (row_count + col_count))
    flattened = flattened[:, : row_count * (row_count + col_count - 1)]
    return jnp.sum(flattened.reshape(head_num, row_count, row_count + col_count - 1), axis=1)


def take_rows(table, index, valid):
    rows = jnp.take(table, index, axis=0)
    shape = (valid.shape[0],) + (1,) * (rows.ndim - 1)
    return jnp.where(valid.reshape(shape), rows, jnp.zeros((), rows.dtype))


def exchange(block):
    return lax.all_to_all(block, "seq", split_axis=0, concat_axis=0, tiled=True)


def local(queries, d_out, neighbour_kv, target, bias):
    tok_rows = queries.shape[1]
    width_dev = queries.shape[2]
    head_count = bias.shape[0]
    head_depth = width_dev // head_count
    stretch_count = tok_rows // STRETCH
    per_owner = 2 * stretch_count
    shard_count = lax.axis_size("seq")
    my_index = lax.axis_index("seq")
    group_rows = tok_rows * shard_count
    seq_stretches = min(SEQ_LEN, group_rows) // STRETCH
    scale_factor = head_depth ** (-0.5)
    bias_rows = bias_grid(bias, STRETCH, NB_LEN).transpose(1, 0, 2)
    row_ids = jnp.arange(STRETCH)
    pair = jnp.stack([queries[0], d_out[0]], axis=1)
    pair_all = lax.all_gather(pair, "seq", axis=0, tiled=True)
    my_targets = target[0]
    slot_count = my_targets.shape[0]
    is_used = my_targets >= 0
    entry = jnp.where(is_used, my_targets, 0)
    stretch_of = entry // 2
    win_rows = stretch_of[:, None] * STRETCH + (STRETCH - 1) + row_ids[None, :]
    in_group = win_rows < group_rows
    win_rows = jnp.minimum(win_rows.reshape(-1), group_rows - 1)
    win = jnp.take(pair_all, win_rows, axis=0).reshape(slot_count, STRETCH, 2, width_dev)
    q_win = win[:, :, 0]
    g_win = win[:, :, 1]
    live_slot = (row_ids[None, :] == 0) | ((stretch_of[:, None] + 1) % seq_stretches != 0)
    q_keep = is_used[:, None] & in_group
    q_slots = jnp.where(q_keep[:, :, None], q_win, jnp.zeros((), q_win.dtype))
    g_slots = jnp.where((q_keep & live_slot)[:, :, None], g_win, jnp.zeros((), g_win.dtype))
    q_slots = q_slots.reshape(slot_count, STRETCH, head_count, head_depth)
    g_slots = g_slots.reshape(slot_count, STRETCH, head_count, head_depth)
    stored = neighbour_kv[0]
    key_rows = stored[:, :, 0].reshape(slot_count, NB_LEN, head_count, head_depth)
    value_rows = stored[:, :, 1].reshape(slot_count, NB_LEN, head_count, head_depth)
    scores = jnp.einsum("sihd,sjhd->sihj", q_slots, key_rows, preferred_element_type=jnp.float32)
    scores = scores * scale_factor + bias_rows[None]
    peak_val = jnp.max(scores, axis=-1)
    weights = jnp.exp(scores - peak_val[..., None])
    row_total = jnp.sum(weights, axis=-1)
    partial_value = jnp.einsum(
        "sihj,sjhd->sihd",
        weights.astype(jnp.bfloat16),
        value_rows,
        preferred_element_type=jnp.float32,
    )
    owner_of = jnp.where(is_used, my_targets // per_owner, -1)
    owner_match = owner_of[None, :] == jnp.arange(shard_count)[:, None]
    send_slot = jnp.argmax(owner_match, axis=1)
    send_has = jnp.any(owner_match, axis=1)
    part_send = take_rows(
        partial_value.astype(jnp.bfloat16).reshape(slot_count, STRETCH, width_dev),
        send_slot,
        send_has,
    )
    g_dot = jnp.einsum(
        "sihd,sihd->sih",
        g_slots.astype(jnp.float32),
        partial_value,
        precision=lax.Precision.HIGHEST,
    )
    mine = jnp.stack([peak_val, row_total, g_dot], axis=1)
    shared = jnp.concatenate(
        [
            mine.reshape(slot_count, -1),
            jnp.where(is_used, entry + 1, 0).astype(jnp.float32)[:, None],
        ],
        axis=1,
    )
    shared_wide = jnp.pad(shared, ((0, 0), (0, 1024 - shared.shape[1])))
    shared_all = lax.all_gather(shared_wide, "seq", tiled=True)[:, : shared.shape[1]]
    partner = entry + 1 - 2 * (entry % 2)
    partner_at = jnp.argmax(
        shared_all[None, :, -1] == (partner + 1).astype(jnp.float32)[:, None], axis=1
    )
    theirs = jnp.take(shared_all[:, :-1], partner_at, axis=0).reshape(mine.shape)
    both_peak = jnp.maximum(mine[:, 0], theirs[:, 0])
    mine_f = jnp.exp(mine[:, 0] - both_peak)
    theirs_f = jnp.exp(theirs[:, 0] - both_peak)
    both_total = mine_f * mine[:, 1] + theirs_f * theirs[:, 1]
    lse_slots = both_peak + jnp.log(both_total)
    dd_slots = (mine_f * mine[:, 2] + theirs_f * theirs[:, 2]) / both_total
    dd_slots = jnp.where(is_used[:, None, None], dd_slots, 0.0)
    part_recv = exchange(part_send)
    own_entries = my_index * per_owner + jnp.arange(per_owner)
    own_at = jnp.argmax(
        shared_all[None, :, -1] == (own_entries + 1).astype(jnp.float32)[:, None], axis=1
    )
    held_by = own_at // slot_count
    parts_own = jnp.take(part_recv, held_by, axis=0).astype(jnp.float32)
    parts_own = parts_own.reshape(stretch_count, 2, STRETCH, head_count, head_depth)
    stats_own = jnp.take(shared_all[:, :-1], own_at, axis=0).reshape(
        stretch_count, 2, 3, STRETCH, head_count
    )
    peaks_own = stats_own[:, :, 0]
    totals_own = stats_own[:, :, 1]
    stretch_ids = my_index * stretch_count + jnp.arange(stretch_count)
    is_live = (row_ids[None, :] == 0) | ((stretch_ids[:, None] + 1) % seq_stretches != 0)
    live_rows = is_live.astype(jnp.float32)
    top_peak = jnp.max(peaks_own, axis=1)
    factor = jnp.exp(peaks_own - top_peak[:, None])
    denominator = jnp.sum(factor * totals_own, axis=1)
    combined = jnp.sum(factor[..., None] * parts_own, axis=1) / denominator[..., None]
    combined = combined * live_rows[:, :, None, None]
    att_win = combined.astype(jnp.bfloat16).reshape(tok_rows, width_dev)
    att_before = passed_along(att_win[tok_rows - STRETCH :], "seq", 1)
    prob_full = jnp.exp(scores - lse_slots[..., None])
    prob_low = prob_full.astype(jnp.bfloat16)
    grad_prob = jnp.einsum(
        "sihd,sjhd->sihj", g_slots, value_rows, preferred_element_type=jnp.float32
    )
    grad_scores = prob_full * (grad_prob - dd_slots[..., None])
    scores_low = grad_scores.astype(jnp.bfloat16)
    grad_rows = (
        jnp.einsum("sihj,sjhd->sihd", scores_low, key_rows, preferred_element_type=jnp.float32)
        * scale_factor
    )
    mix_probs = jnp.stack([scores_low, prob_low], axis=1)
    mix_rows = jnp.stack([q_slots, g_slots], axis=1)
    grad_kv = jnp.einsum(
        "sxihj,sxihd->sjxhd", mix_probs, mix_rows, preferred_element_type=jnp.float32
    )
    kv_scale = jnp.array([scale_factor, 1.0], jnp.float32)[None, None, :, None, None]
    d_kv = (grad_kv * kv_scale).astype(jnp.bfloat16).reshape(slot_count, NB_LEN, 2, width_dev)
    bias_part = bias_fold(jnp.sum(grad_scores, axis=0).transpose(1, 0, 2))
    dq_rows = jnp.zeros((shard_count, stretch_count, STRETCH, width_dev), jnp.bfloat16)
    dq_owner = jnp.where(is_used, owner_of, shard_count)
    dq_rows = dq_rows.at[dq_owner, stretch_of % stretch_count].set(
        grad_rows.astype(jnp.bfloat16).reshape(slot_count, STRETCH, width_dev), mode="drop"
    )
    grad_win = lax.psum_scatter(dq_rows, "seq", scatter_dimension=0, tiled=True)
    grad_win = grad_win.reshape(tok_rows, width_dev)
    grad_before = passed_along(grad_win[tok_rows - STRETCH :], "seq", 1)
    attended = jnp.concatenate([att_before[1:], att_win[: tok_rows - STRETCH + 1]])
    d_query = jnp.concatenate([grad_before[1:], grad_win[: tok_rows - STRETCH + 1]])
    raw_sum = lax.psum(lax.psum(bias_part, "seq"), "grp")
    squares = lax.psum(jnp.sum(raw_sum * raw_sum), "mp")
    d_bias = raw_sum * jnp.minimum(1.0, 1.0 / jnp.sqrt(squares + 1e-12))
    return (attended[None], d_query[None], d_kv[None], d_bias)


def solution(mesh):
    in_specs = (
        P("grp", "seq", "mp"),
        P("grp", "seq", "mp"),
        P("grp", "seq", None, None, "mp"),
        P("grp", "seq"),
        P("mp", None),
    )
    out_specs = (
        P("grp", "seq", "mp"),
        P("grp", "seq", "mp"),
        P("grp", "seq", None, None, "mp"),
        P("mp", None),
    )
    return jax.shard_map(local, mesh=mesh, in_specs=in_specs, out_specs=out_specs, check_vma=False)
```

profile of v0, /device:TPU:1, one launch (start us, length us, event | category | flops | bytes accessed | tf_op | source)
XLA Modules:
  0.0 341.9 jit_solution(12824938684409181369)
XLA Ops:
  7.2 1.1 pad_maximum_fusion.1
  8.4 1.0 copy.104
  10.3 0.7 copy.111
  11.0 0.7 pad.16
  12.3 3.8 %copy.106 = bf16[1,8,128,2,512]{2,4,1,3,0:T(8,128)(2,1)} copy(bf16[1,8,128,2,512]{4,3,2,1,0:T(2,128)(2,1)S(1)} %copy-done.8) | data formatting | bytes 4194304 | tf_op args[2]
  16.9 2.8 fusion.54
  19.7 75.7 %all-gather.3.cloned.1.call-done = bf16[4096,2,512]{2,1,0:T(2,128)(2,1)} async-done(((bf16[128,2,512]{2,1,0:T(2,128)(2,1)}), bf16[4096,2,512]{2,1,0:T(2,128)(2,1)}) %all-gather.3.cloned.1.call-update) | async-done | bytes 8388624 | tf_op jit(solution)/shard_map/all_gather | solution.py:61
  95.4 6.4 %gather_fusion = bf16[512,2,512]{2,1,0:T(2,128)(2,1)S(1)} fusion(bf16[4096,2,512]{2,1,0:T(2,128)(2,1)} %all-gather.3.cloned.1.call-done, s32[1024]{0:T(1024)S(1)} %pad_clamp_fusion.4), kind=kCustom, calls=%fused_computation | custom fusion | bytes 2099200 | tf_op jit(solution)/shard_map/jit(_take)/gather | solution.py:70
  102.4 0.7 broadcast_select_fusion.1
  103.1 1.4 fusion.53
  105.1 2.0 multiply_reduce_fusion
  108.9 1.1 copy.160
  110.1 2.0 gather_fusion.2
  112.1 3.3 select_select_fusion
  115.3 7.8 %all-to-all-start = ((bf16[32,64,512]{2,1,0:T(8,128)(2,1)}), bf16[32,64,512]{2,1,0:T(8,128)(2,1)}, u32[]{:S(2)}, u32[]{:S(2)}) async-start(bf16[32,64,512]{2,1,0:T(8,128)(2,1)} %select_select_fusion), calls=%async_computation | async-start | bytes 4194304 | tf_op jit(solution)/shard_map/all_to_all | solution.py:43
  123.2 76.4 %all-gather.5.cloned.1.call-done = f32[256,1024]{1,0:T(8,128)} async-done(((f32[8,1024]{1,0:T(8,128)}), f32[256,1024]{1,0:T(8,128)}) %all-gather.5.cloned.1.call-update) | async-done | bytes 1048592 | tf_op jit(solution)/shard_map/all_gather | solution.py:117
  199.6 1.0 slice_reduce_fusion
  200.6 0.7 iota_reduce_fusion
  201.9 2.1 slice.108
  203.9 2.3 gather_fusion.4
  206.2 0.9 copy.120
  207.2 0.8 copy.121
  207.9 1.0 broadcast_select_fusion.3
  208.9 0.8 log_add_fusion
  209.7 0.8 fusion.3
  210.5 1.0 copy-done
  211.5 0.8 fusion.5
  212.4 2.4 broadcast_in_dim.169
  214.9 2.5 scatter_fusion
  218.4 0.9 squeeze.45
  219.3 1.0 squeeze.44
  220.3 1.0 fusion.55
  222.0 45.5 %psum.21 = f32[4,191]{1,0:T(4,128)S(1)} all-reduce(f32[4,191]{1,0:T(4,128)S(1)} %reduce_sum.58), channel_id=1, replica_groups=mesh['grp'=4,'seq'=32,'mp'=4] {'seq'}, use_global_device_ids=true, to_apply=%region_13.14 | all-reduce | flops 764 | bytes 6112 | tf_op jit(solution)/shard_map/psum | solution.py:182
  267.5 8.4 %psum.22 = f32[4,191]{1,0:T(4,128)S(1)} all-reduce(f32[4,191]{1,0:T(4,128)S(1)} %psum.21), channel_id=1, replica_groups=mesh['grp'=4,'seq'=32,'mp'=4] {'grp'}, use_global_device_ids=true, to_apply=%region_14.15 | all-reduce | flops 764 | bytes 6112 | tf_op jit(solution)/shard_map/psum | solution.py:182
  276.5 1.2 copy_select_fusion.1
  277.7 10.2 %psum.23 = f32[]{:T(128)} all-reduce(f32[]{:T(128)} %multiply_reduce_fusion.2), channel_id=1, replica_groups=mesh['grp'=4,'seq'=32,'mp'=4] {'mp'}, use_global_device_ids=true, to_apply=%region_16.17 | all-reduce | flops 1 | bytes 8 | tf_op jit(solution)/shard_map/psum | solution.py:183
  287.9 0.7 iota_reduce_fusion.2
  289.9 1.7 gather_fusion.1
  293.0 2.2 multiply_convert_fusion
  295.2 3.8 %copy.129 = bf16[1,8,128,2,512]{4,3,2,1,0:T(2,128)(2,1)} copy(bf16[1,8,128,2,512]{2,4,3,1,0:T(8,128)(2,1)S(1)} %bitcast.165) | data formatting | bytes 4194304
  299.8 2.2 gather_fusion.3
  302.9 5.1 %collective-permute-start = (bf16[64,512]{1,0:T(8,128)(2,1)S(1)}, bf16[64,512]{1,0:T(8,128)(2,1)S(1)}, u32[]{:S(2)}, u32[]{:S(2)}) collective-permute-start(bf16[64,512]{1,0:T(8,128)(2,1)S(1)} %bitcast.180), channel_id=1, source_target_pairs={{0,4},{4,8},{8,12},{12,16},{16,20},{20,24},{24,28},{28,32},{32,36}... | collective-permute-start | bytes 196616 | tf_op jit(solution)/shard_map/ppermute | solution.py:14
  308.2 1.9 collective-permute-done
  310.1 18.2 %reduce-scatter.2.cloned.1.call-done = bf16[1,2,64,512]{3,2,1,0:T(8,128)(2,1)} async-done(((bf16[32,2,64,512]{3,2,1,0:T(8,128)(2,1)}), bf16[1,2,64,512]{3,2,1,0:T(8,128)(2,1)}) %reduce-scatter.2.cloned.1.call-update) | async-done | bytes 131088 | tf_op jit(solution)/shard_map/reduce_scatter | solution.py:177
  328.3 0.8 slice_bitcast_fusion.1
  329.1 3.4 collective-permute-start.1
  332.6 0.7 maximum_bitcast_fusion
  333.2 0.9 slice.121
  (133 shorter events, 13.0 us)
Async XLA Ops:
  7.2 5.2 %copy-start.8 = (bf16[1,8,128,2,512]{4,3,2,1,0:T(2,128)(2,1)S(1)}, bf16[1,8,128,2,512]{4,3,2,1,0:T(2,128)(2,1)}, u32[]{:S(2)}) copy-start(bf16[1,8,128,2,512]{4,3,2,1,0:T(2,128)(2,1)} %param.8) | copy-start | bytes 6291460
  7.2 88.3 %all-gather.3.cloned.1.call-start = ((), (), s32[]{:S(2)}) async-start(), calls=%async_computation.2 | async-start | bytes 8650752 | tf_op jit(solution)/shard_map/all_gather | solution.py:61
  9.4 190.3 %all-gather.5.cloned.1.call-start = ((), (), s32[]{:S(2)}) async-start(), calls=%async_computation.3 | async-start | bytes 1081344 | tf_op jit(solution)/shard_map/all_gather | solution.py:117
  10.1 6.1 %copy-start.21 = (pred[8]{0:T(512)(128)(4,1)}, pred[8]{0:T(512)(128)(4,1)S(1)}, u32[]{:S(2)}) copy-start(pred[8]{0:T(512)(128)(4,1)S(1)} %get-tuple-element.54) | copy-start | bytes 28
  16.1 3.6 %copy-start.23 = (pred[64]{0:T(512)(128)(4,1)}, pred[64]{0:T(512)(128)(4,1)S(1)}, u32[]{:S(2)}) copy-start(pred[64]{0:T(512)(128)(4,1)S(1)} %iota_compare_fusion.2) | copy-start | bytes 196
  16.2 86.1 %copy-start.17 = (pred[8,64]{1,0:T(8,128)(4,1)}, pred[8,64]{1,0:T(8,128)(4,1)S(1)}, u32[]{:S(2)}) copy-start(pred[8,64]{1,0:T(8,128)(4,1)S(1)} %get-tuple-element.51) | copy-start | bytes 1540
  16.2 86.9 %copy-start.15 = (pred[8,64]{1,0:T(8,128)(4,1)}, pred[8,64]{1,0:T(8,128)(4,1)S(1)}, u32[]{:S(2)}) copy-start(pred[8,64]{1,0:T(8,128)(4,1)S(1)} %get-tuple-element.50) | copy-start | bytes 1540
  102.1 2.5 copy-start.4
  102.4 2.2 copy-start.2
  105.1 3.1 copy-start.22
  107.1 1.8 copy-start.12
  107.1 1.8 copy-start.13
  115.3 184.5 %all-to-all-start = ((bf16[32,64,512]{2,1,0:T(8,128)(2,1)}), bf16[32,64,512]{2,1,0:T(8,128)(2,1)}, u32[]{:S(2)}, u32[]{:S(2)}) async-start(bf16[32,64,512]{2,1,0:T(8,128)(2,1)} %select_select_fusion), calls=%async_computation | async-start | bytes 4194304 | tf_op jit(solution)/shard_map/all_to_all | solution.py:43
  123.2 86.5 %copy-start.9 = (bf16[8,64,4,128]{3,2,1,0:T(4,128)(2,1)S(1)}, bf16[8,64,4,128]{3,2,1,0:T(4,128)(2,1)}, u32[]{:S(2)}) copy-start(bf16[8,64,4,128]{3,2,1,0:T(4,128)(2,1)} %get-tuple-element.35) | copy-start | bytes 1572868
  123.2 205.1 %reduce-scatter.2.cloned.1.call-start = ((), (), s32[]{:S(2)}) async-start(), calls=%async_computation.4 | async-start | bytes 4325376 | tf_op jit(solution)/shard_map/reduce_scatter | solution.py:177
  200.6 3.3 copy-start.19
  207.9 3.5 %copy-start.3 = (bf16[8,128,1,512]{1,3,0,2:T(8,128)(2,1)S(1)}, bf16[8,128,1,512]{1,3,0,2:T(8,128)(2,1)}, u32[]{:S(2)}) copy-start(bf16[8,128,1,512]{1,3,0,2:T(8,128)(2,1)} %get-tuple-element.38) | copy-start | bytes 3145732
  209.7 2.6 copy-start.10
  210.5 1.0 copy-start
  212.4 2.4 copy-start.14
  217.4 0.7 copy-start.24
  217.4 1.0 copy-start.5
  217.4 3.0 copy-start.1
  219.3 57.2 %copy-start.6 = (bf16[8,1,64,4,128]{4,3,2,0,1:T(4,128)(2,1)S(1)}, bf16[8,1,64,4,128]{4,3,2,0,1:T(4,128)(2,1)}, u32[]{:S(2)}) copy-start(bf16[8,1,64,4,128]{4,3,2,0,1:T(4,128)(2,1)} %squeeze.45) | copy-start | bytes 1572868
  219.3 57.2 %copy-start.16 = (pred[8,64]{1,0:T(8,128)(4,1)S(1)}, pred[8,64]{1,0:T(8,128)(4,1)}, u32[]{:S(2)}) copy-start(pred[8,64]{1,0:T(8,128)(4,1)} %copy-done.15) | copy-start | bytes 1540
  219.3 57.2 %copy-start.18 = (pred[8,64]{1,0:T(8,128)(4,1)S(1)}, pred[8,64]{1,0:T(8,128)(4,1)}, u32[]{:S(2)}) copy-start(pred[8,64]{1,0:T(8,128)(4,1)} %copy-done.17) | copy-start | bytes 1540
  220.3 56.2 %copy-start.7 = (bf16[8,1,64,4,128]{4,3,2,0,1:T(4,128)(2,1)S(1)}, bf16[8,1,64,4,128]{4,3,2,0,1:T(4,128)(2,1)}, u32[]{:S(2)}) copy-start(bf16[8,1,64,4,128]{4,3,2,0,1:T(4,128)(2,1)} %squeeze.44) | copy-start | bytes 1572868
  221.3 66.6 %copy-start.20 = (f32[256]{0:T(256)S(1)}, f32[256]{0:T(256)}, u32[]{:S(2)}) copy-start(f32[256]{0:T(256)} %copy-done.19) | copy-start | bytes 3076
  221.4 71.2 %copy-start.11 = (f32[8,64,4]{1,2,0:T(4,128)S(1)}, f32[8,64,4]{1,2,0:T(4,128)}, u32[]{:S(2)}) copy-start(f32[8,64,4]{1,2,0:T(4,128)} %copy-done.10) | copy-start | bytes 24580
  295.2 3.8 %copy-start.26 = (pred[2,2]{1,0:T(4,128)(4,1)S(1)}, pred[2,2]{1,0:T(4,128)(4,1)}, u32[]{:S(2)}) copy-start(pred[2,2]{1,0:T(4,128)(4,1)} %broadcast_in_dim.155) | copy-start | bytes 16
  299.0 3.0 copy-start.25
  302.9 7.1 %collective-permute-start = (bf16[64,512]{1,0:T(8,128)(2,1)S(1)}, bf16[64,512]{1,0:T(8,128)(2,1)S(1)}, u32[]{:S(2)}, u32[]{:S(2)}) collective-permute-start(bf16[64,512]{1,0:T(8,128)(2,1)S(1)} %bitcast.180), channel_id=1, source_target_pairs={{0,4},{4,8},{8,12},{12,16},{16,20},{20,24},{24,28},{28,32},{32,36}... | collective-permute-start | bytes 196616 | tf_op jit(solution)/shard_map/ppermute | solution.py:14
  329.1 5.5 %collective-permute-start.1 = (bf16[64,512]{1,0:T(8,128)(2,1)S(1)}, bf16[64,512]{1,0:T(8,128)(2,1)S(1)}, u32[]{:S(2)}, u32[]{:S(2)}) collective-permute-start(bf16[64,512]{1,0:T(8,128)(2,1)S(1)} %slice_bitcast_fusion.1), channel_id=1, source_target_pairs={{0,4},{4,8},{8,12},{12,16},{16,20},{20,24},{24,28},{28,32},{32,36}... | collective-permute-start | bytes 196616 | tf_op jit(solution)/shard_map/ppermute | solution.py:14
Sparse Core Ops, SparseCore 0:
  10.1 85.2 all-gather.2
  108.3 91.2 all-gather.4
  217.5 110.7 reduce-scatter.1
where the time goes:
time: 343 us; the launch traced here: 342 us
  waiting for transfers between devices  173 us (50%)
  blocking collectives  64.2 us (19%)
  local copies, waits for them, and re-layouts  47.5 us (14%)
  other arithmetic  19.6 us (6%)
  starting transfers between devices  16.5 us (5%)
  between operations  15 us (4%)
  matrix products  6.32 us (2%)
    all_gather x1, waiting for transfers between devices, local(): lax.all_gather(shared_wide, 'seq', tiled=True)[:, :shared.shape[1]]  76.4 us
    all_gather x1, waiting for transfers between devices, local(): pair_all = lax.all_gather(pair, 'seq', axis=0, tiled=True)  75.7 us
    psum x2, blocking collectives, local(): raw_sum = lax.psum(lax.psum(bias_part, 'seq'), 'grp')  53.9 us
    reduce_scatter x1, waiting for transfers between devices, local(): grad_win = lax.psum_scatter(dq_rows, 'seq', scatter_dimension=0, tiled=True)  18.2 us
    psum x1, blocking collectives, local(): squares = lax.psum(jnp.sum(raw_sum * raw_sum), 'mp')  10.2 us
    unnamed x58, local copies, waits for them, and re-layouts  9.33 us
    ppermute x2, starting transfers between devices, passed_along(): return lax.ppermute(block, axis, route)  8.55 us
    all_to_all x1, starting transfers between devices, exchange(): return lax.all_to_all(block, 'seq', split_axis=0, concat_axis=0, tiled=True)  7.84 us
  transfers between devices with their start and end apart: 6, of which 5 were waited for; matrix products, arithmetic and copies ran while one was open for 16% of the time, Pallas kernels for 0%

commit v1 on v0

--- a/solution.py
+++ b/solution.py
@@ -58,7 +58,9 @@
     bias_rows = bias_grid(bias, STRETCH, NB_LEN).transpose(1, 0, 2)
     row_ids = jnp.arange(STRETCH)
     pair = jnp.stack([queries[0], d_out[0]], axis=1)
-    pair_all = lax.all_gather(pair, "seq", axis=0, tiled=True)
+    pair_all = jnp.concatenate(
+        jax.lax.all_to_all(jnp.stack(jax.lax.axis_size("seq") * [pair], 0), "seq", 0, 0), 0
+    )
     my_targets = target[0]
     slot_count = my_targets.shape[0]
     is_used = my_targets >= 0

time: 343 us -> 649 us (1.89)
  waiting for transfers between devices: 173 us -> 450 us
  starting transfers between devices: 16.5 us -> 39.2 us
  local copies, waits for them, and re-layouts: 47.5 us -> 54.7 us
    all_to_all x0 -> x1, waiting for transfers between devices: none -> 352 us  [local(): jax.lax.all_to_all(jnp.stack(jax.lax.axis_size('seq') * [pair], 0), 'seq'...]
    all_gather x1 -> x0, waiting for transfers between devices: 75.7 us -> none  [local(): pair_all = lax.all_gather(pair, 'seq', axis=0, tiled=True)]
    all_to_all x0 -> x1, starting transfers between devices: none -> 16.9 us  [local(): jax.lax.all_to_all(jnp.stack(jax.lax.axis_size('seq') * [pair], 0), 'seq'...]
    another operation x0 -> x1, local copies, waits for them, and re-layouts: none -> 8.68 us  [local(): jnp.stack(jax.lax.axis_size('seq') * [pair], 0)]
  transfers between devices with their start and end apart: 6 -> 6, of which waited for: 5 -> 5; matrix products, arithmetic and copies ran while one was open for 16% -> 8% of each run, Pallas kernels for 0% -> 0%
where the time goes in v1:
time: 649 us; the launch traced here: 648 us
  waiting for transfers between devices  450 us (69%)
  blocking collectives  63.6 us (10%)
  local copies, waits for them, and re-layouts  54.7 us (8%)
  starting transfers between devices  39.2 us (6%)
  other arithmetic  18.8 us (3%)
  between operations  15.3 us (2%)
    all_to_all x1, waiting for transfers between devices, local(): jax.lax.all_to_all(jnp.stack(jax.lax.axis_size('seq') * [pair], 0), 'seq'...  352 us
    all_gather x1, waiting for transfers between devices, local(): lax.all_gather(shared_wide, 'seq', tiled=True)[:, :shared.shape[1]]  77.9 us
    psum x2, blocking collectives, local(): raw_sum = lax.psum(lax.psum(bias_part, 'seq'), 'grp')  54.5 us
    reduce_scatter x1, waiting for transfers between devices, local(): grad_win = lax.psum_scatter(dq_rows, 'seq', scatter_dimension=0, tiled=True)  17.8 us
    all_to_all x1, starting transfers between devices, local(): jax.lax.all_to_all(jnp.stack(jax.lax.axis_size('seq') * [pair], 0), 'seq'...  16.9 us
  transfers between devices with their start and end apart: 6, of which 5 were waited for; matrix products, arithmetic and copies ran while one was open for 8% of the time, Pallas kernels for 0%

profile of v1, /device:TPU:1, one launch (start us, length us, event | category | flops | bytes accessed | tf_op | source)
XLA Modules:
  0.0 647.8 jit_solution(11398642001018481064)
XLA Ops:
  7.2 1.0 pad_maximum_fusion.1
  8.4 8.7 %stack.21 = bf16[32,128,2,512]{3,2,1,0:T(2,128)(2,1)} broadcast(bf16[128,2,512]{2,1,0:T(2,128)(2,1)S(1)} %copy.104), dimensions={1,2,3} | broadcast | bytes 8650752 | tf_op jit(solution)/shard_map/stack | solution.py:62
  17.1 16.9 %all-to-all-start = ((bf16[32,128,2,512]{3,2,1,0:T(2,128)(2,1)}), bf16[32,128,2,512]{3,2,1,0:T(2,128)(2,1)}, u32[]{:S(2)}, u32[]{:S(2)}) async-start(bf16[32,128,2,512]{3,2,1,0:T(2,128)(2,1)} %stack.21), calls=%async_computation | async-start | bytes 16777216 | tf_op jit(solution)/shard_map/all_to_all | solution.py:62
  35.7 3.8 copy.106
  40.3 2.7 fusion.54
  43.0 351.6 %all-to-all-done = bf16[32,128,2,512]{3,2,1,0:T(2,128)(2,1)} async-done(((bf16[32,128,2,512]{3,2,1,0:T(2,128)(2,1)}), bf16[32,128,2,512]{3,2,1,0:T(2,128)(2,1)}, u32[]{:S(2)}, u32[]{:S(2)}) %all-to-all-start) | async-done | bytes 8388640 | tf_op jit(solution)/shard_map/all_to_all | solution.py:62
  394.7 6.4 gather_fusion
  401.6 1.4 fusion.53
  403.1 0.7 broadcast_select_fusion.1
  404.3 2.0 multiply_reduce_fusion
  408.1 1.1 copy.160
  409.3 2.0 gather_fusion.2
  411.3 3.3 select_select_fusion
  414.5 12.9 %all-to-all-start.1 = ((bf16[32,64,512]{2,1,0:T(8,128)(2,1)}), bf16[32,64,512]{2,1,0:T(8,128)(2,1)}, u32[]{:S(2)}, u32[]{:S(2)}) async-start(bf16[32,64,512]{2,1,0:T(8,128)(2,1)} %select_select_fusion), calls=%async_computation.1 | async-start | bytes 4194304 | tf_op jit(solution)/shard_map/all_to_all | solution.py:43
  427.5 77.9 %all-gather.2.cloned.1.call-done = f32[256,1024]{1,0:T(8,128)} async-done(((f32[8,1024]{1,0:T(8,128)}), f32[256,1024]{1,0:T(8,128)}) %all-gather.2.cloned.1.call-update) | async-done | bytes 1048592 | tf_op jit(solution)/shard_map/all_gather | solution.py:119
  505.4 1.0 slice_reduce_fusion
  506.4 0.7 iota_reduce_fusion
  507.7 2.1 slice.108
  509.8 2.3 gather_fusion.4
  512.1 0.9 copy.120
  513.0 0.8 copy.121
  513.8 1.0 broadcast_select_fusion.3
  514.8 0.8 log_add_fusion
  515.6 0.8 fusion.3
  516.4 1.0 copy-done
  517.3 0.8 fusion.5
  518.3 2.4 broadcast_in_dim.169
  520.7 2.5 scatter_fusion
  524.2 0.9 squeeze.45
  525.2 0.9 squeeze.44
  526.1 1.0 fusion.55
  527.7 45.7 %psum.21 = f32[4,191]{1,0:T(4,128)S(1)} all-reduce(f32[4,191]{1,0:T(4,128)S(1)} %reduce_sum.58), channel_id=1, replica_groups=mesh['grp'=4,'seq'=32,'mp'=4] {'seq'}, use_global_device_ids=true, to_apply=%region_13.14 | all-reduce | flops 764 | bytes 6112 | tf_op jit(solution)/shard_map/psum | solution.py:184
  573.4 8.8 %psum.22 = f32[4,191]{1,0:T(4,128)S(1)} all-reduce(f32[4,191]{1,0:T(4,128)S(1)} %psum.21), channel_id=1, replica_groups=mesh['grp'=4,'seq'=32,'mp'=4] {'grp'}, use_global_device_ids=true, to_apply=%region_14.15 | all-reduce | flops 764 | bytes 6112 | tf_op jit(solution)/shard_map/psum | solution.py:184
  582.8 1.2 copy_select_fusion.1
  584.0 9.1 %psum.23 = f32[]{:T(128)} all-reduce(f32[]{:T(128)} %multiply_reduce_fusion.2), channel_id=1, replica_groups=mesh['grp'=4,'seq'=32,'mp'=4] {'mp'}, use_global_device_ids=true, to_apply=%region_16.17 | all-reduce | flops 1 | bytes 8 | tf_op jit(solution)/shard_map/psum | solution.py:185
  593.1 0.7 iota_reduce_fusion.2
  593.8 1.7 gather_fusion.1
  597.5 2.2 multiply_convert_fusion
  599.8 3.8 copy.129
  605.0 2.2 gather_fusion.3
  608.1 5.7 collective-permute-start
  614.0 1.9 collective-permute-done
  615.9 17.8 %reduce-scatter.2.cloned.1.call-done = bf16[1,2,64,512]{3,2,1,0:T(8,128)(2,1)} async-done(((bf16[32,2,64,512]{3,2,1,0:T(8,128)(2,1)}), bf16[1,2,64,512]{3,2,1,0:T(8,128)(2,1)}) %reduce-scatter.2.cloned.1.call-update) | async-done | bytes 131088 | tf_op jit(solution)/shard_map/reduce_scatter | solution.py:179
  633.7 0.8 slice_bitcast_fusion.1
  634.5 3.6 collective-permute-start.1
  638.1 0.7 maximum_bitcast_fusion
  638.8 0.9 slice.121
  640.3 0.7 maximum_bitcast_fusion.1
  (135 shorter events, 12.6 us)
Async XLA Ops:
  17.1 17.0 %copy-start.23 = (s32[1,8]{1,0:T(1,128)S(1)}, s32[1,8]{1,0:T(1,128)}, u32[]{:S(2)}) copy-start(s32[1,8]{1,0:T(1,128)} %param.9) | copy-start | bytes 100
  17.1 17.2 %copy-start.22 = (f32[4,191]{1,0:T(4,128)S(1)}, f32[4,191]{1,0:T(4,128)}, u32[]{:S(2)}) copy-start(f32[4,191]{1,0:T(4,128)} %param.10) | copy-start | bytes 9172
  17.1 377.5 %all-to-all-start = ((bf16[32,128,2,512]{3,2,1,0:T(2,128)(2,1)}), bf16[32,128,2,512]{3,2,1,0:T(2,128)(2,1)}, u32[]{:S(2)}, u32[]{:S(2)}) async-start(bf16[32,128,2,512]{3,2,1,0:T(2,128)(2,1)} %stack.21), calls=%async_computation | async-start | bytes 16777216 | tf_op jit(solution)/shard_map/all_to_all | solution.py:62
  34.1 1.6 copy-start.8
  34.1 471.3 %all-gather.2.cloned.1.call-start = ((), (), s32[]{:S(2)}) async-start(), calls=%async_computation.3 | async-start | bytes 1081344 | tf_op jit(solution)/shard_map/all_gather | solution.py:119
  34.2 5.4 copy-start.21
  39.5 3.5 copy-start.24
  39.6 362.0 %copy-start.15 = (pred[8,64]{1,0:T(8,128)(4,1)}, pred[8,64]{1,0:T(8,128)(4,1)S(1)}, u32[]{:S(2)}) copy-start(pred[8,64]{1,0:T(8,128)(4,1)S(1)} %get-tuple-element.50) | copy-start | bytes 1540
  39.7 363.4 %copy-start.17 = (pred[8,64]{1,0:T(8,128)(4,1)}, pred[8,64]{1,0:T(8,128)(4,1)S(1)}, u32[]{:S(2)}) copy-start(pred[8,64]{1,0:T(8,128)(4,1)S(1)} %get-tuple-element.51) | copy-start | bytes 1540
  401.3 1.7 copy-start.4
  401.6 2.2 copy-start.2
  406.3 1.8 copy-start.12
  406.3 1.8 copy-start.13
  414.5 190.5 %all-to-all-start.1 = ((bf16[32,64,512]{2,1,0:T(8,128)(2,1)}), bf16[32,64,512]{2,1,0:T(8,128)(2,1)}, u32[]{:S(2)}, u32[]{:S(2)}) async-start(bf16[32,64,512]{2,1,0:T(8,128)(2,1)} %select_select_fusion), calls=%async_computation.1 | async-start | bytes 4194304 | tf_op jit(solution)/shard_map/all_to_all | solution.py:43
  427.4 88.2 %copy-start.9 = (bf16[8,64,4,128]{3,2,1,0:T(4,128)(2,1)S(1)}, bf16[8,64,4,128]{3,2,1,0:T(4,128)(2,1)}, u32[]{:S(2)}) copy-start(bf16[8,64,4,128]{3,2,1,0:T(4,128)(2,1)} %get-tuple-element.35) | copy-start | bytes 1572868
  427.4 206.3 %reduce-scatter.2.cloned.1.call-start = ((), (), s32[]{:S(2)}) async-start(), calls=%async_computation.4 | async-start | bytes 4325376 | tf_op jit(solution)/shard_map/reduce_scatter | solution.py:179
  506.4 3.4 copy-start.19
  513.8 3.5 copy-start.3
  515.6 2.6 copy-start.10
  516.4 1.0 copy-start
  518.3 2.4 copy-start.14
  523.2 0.7 copy-start.25
  523.2 1.0 copy-start.5
  523.2 2.9 copy-start.1
  525.2 57.6 %copy-start.6 = (bf16[8,1,64,4,128]{4,3,2,0,1:T(4,128)(2,1)S(1)}, bf16[8,1,64,4,128]{4,3,2,0,1:T(4,128)(2,1)}, u32[]{:S(2)}) copy-start(bf16[8,1,64,4,128]{4,3,2,0,1:T(4,128)(2,1)} %squeeze.45) | copy-start | bytes 1572868
  525.2 57.6 %copy-start.16 = (pred[8,64]{1,0:T(8,128)(4,1)S(1)}, pred[8,64]{1,0:T(8,128)(4,1)}, u32[]{:S(2)}) copy-start(pred[8,64]{1,0:T(8,128)(4,1)} %copy-done.15) | copy-start | bytes 1540
  525.2 57.6 %copy-start.18 = (pred[8,64]{1,0:T(8,128)(4,1)S(1)}, pred[8,64]{1,0:T(8,128)(4,1)}, u32[]{:S(2)}) copy-start(pred[8,64]{1,0:T(8,128)(4,1)} %copy-done.17) | copy-start | bytes 1540
  526.1 56.7 %copy-start.7 = (bf16[8,1,64,4,128]{4,3,2,0,1:T(4,128)(2,1)S(1)}, bf16[8,1,64,4,128]{4,3,2,0,1:T(4,128)(2,1)}, u32[]{:S(2)}) copy-start(bf16[8,1,64,4,128]{4,3,2,0,1:T(4,128)(2,1)} %squeeze.44) | copy-start | bytes 1572868
  527.1 66.1 %copy-start.20 = (f32[256]{0:T(256)S(1)}, f32[256]{0:T(256)}, u32[]{:S(2)}) copy-start(f32[256]{0:T(256)} %copy-done.19) | copy-start | bytes 3076
  527.2 70.0 %copy-start.11 = (f32[8,64,4]{1,2,0:T(4,128)S(1)}, f32[8,64,4]{1,2,0:T(4,128)}, u32[]{:S(2)}) copy-start(f32[8,64,4]{1,2,0:T(4,128)} %copy-done.10) | copy-start | bytes 24580
  599.7 4.5 copy-start.27
  603.6 3.7 copy-start.26
  608.1 7.7 %collective-permute-start = (bf16[64,512]{1,0:T(8,128)(2,1)S(1)}, bf16[64,512]{1,0:T(8,128)(2,1)S(1)}, u32[]{:S(2)}, u32[]{:S(2)}) collective-permute-start(bf16[64,512]{1,0:T(8,128)(2,1)S(1)} %bitcast.180), channel_id=1, source_target_pairs={{0,4},{4,8},{8,12},{12,16},{16,20},{20,24},{24,28},{28,32},{32,36}... | collective-permute-start | bytes 196616 | tf_op jit(solution)/shard_map/ppermute | solution.py:14
  634.5 5.7 collective-permute-start.1
Sparse Core Ops, SparseCore 0:
  407.5 97.8 all-gather.1
  523.3 110.3 reduce-scatter.1
